TPU v7x, 32 devices: a whole 2x2x4 slice. The times are simulated.
32 devices in a mesh: occ: 4 (over z), vir: 8 (over y, x, core).
Axes of the slice: x: 2, y: 2, z: 4, core: 2. Of those that a mesh axis runs over, the one named last changes fastest.
Arguments:
- lam: bfloat16 [4096, 12288], P('occ', 'vir'), may hold values from -6 to 6
- integrals: bfloat16 [12288, 1024], P('vir', 'occ'), may hold values from -0.21875 to 0.21875
- occ_sym: int32 [32], P('occ'), may hold values from 0 to 7, as said below
- cd_sym: int32 [96], P('vir'), may hold values from 0 to 7
- ab_sym: int32 [8], replicated, may hold values from 0 to 7
Outputs:
- ladder: bfloat16 [4096, 1024], P('occ', 'vir')
Inputs may be any that keep to these rules, and one draw needn't show every extreme that they name: `occ_sym`: in each aligned block of 8 tiles (those of one index of occ) each representation labels the same number of tiles, 1 of them.
All inputs are finite; a program needn't handle non-finite values.
Results may differ from a plain program's by a relative error of at most 0.001.
Values may be sent and summed in bfloat16 or wider, within the bound.
No kernel may reach another device: no remote copies, remote signals or barrier semaphores. Data moves between devices by JAX's collectives and lax.ppermute only.
A program may use at most 128 MiB of HBM per device.

v0:
```python
import jax
import jax.numpy as jnp
from jax import lax
from jax.sharding import PartitionSpec as P


def halving_reduce_scatter(parts, axis):
    n = lax.axis_size(axis)
    me = lax.axis_index(axis)
    step = 1
    while step < n:
        bit = (me // step) % 2
        pairs = parts.reshape(parts.shape[0] // 2, 2, *parts.shape[1:])
        keep = lax.dynamic_index_in_dim(pairs, bit, axis=1, keepdims=False)
        send = lax.dynamic_index_in_dim(pairs, 1 - bit, axis=1, keepdims=False)
        perm = [(j, j ^ step) for j in range(n)]
        parts = keep + lax.ppermute(send, axis, perm)
        step *= 2
    return parts[0]


def doubling_max(value, axis):
    n = lax.axis_size(axis)
    step = 1
    while step < n:
        value = jnp.maximum(value, lax.ppermute(value, axis, [(j, j ^ step) for j in range(n)]))
        step *= 2
    return value


def packed_partials(lam_kept, int_kept, order, valid, col_of, col_tiles, cap):
    peers = order.shape[0]
    received = lax.all_gather(int_kept[:cap], "occ", axis=0, tiled=True)
    q = order[:, :cap].reshape(-1)
    t = col_of.reshape(peers, -1)[:, :cap].reshape(-1)
    ok = valid[:, :cap].reshape(-1)
    lam_tiles = jnp.where(ok[:, None, None], lam_kept[q], jnp.zeros((), lam_kept.dtype))
    products = jnp.einsum(
        "srm,smc->src", lam_tiles, received, preferred_element_type=jnp.float32
    )
    owner = (t[None, :] == jnp.arange(col_tiles)[:, None]) & ok[None, :]
    return jnp.einsum(
        "ts,src->trc", owner.astype(jnp.float32), products, precision=lax.Precision.HIGHEST
    )


def on_device(lam, integrals, occ_sym, cd_sym, ab_sym):
    row_tiles = occ_sym.shape[0]
    cd_tiles = cd_sym.shape[0]
    tile_edge = lam.shape[0] // row_tiles
    col_tiles = ab_sym.shape[0]
    own_cols = integrals.shape[1] // tile_edge
    peers = col_tiles // own_cols
    row_of = jnp.argmax(occ_sym[None, :] == ab_sym[:, None], axis=1)
    kept = cd_sym[:, None] == ab_sym[None, :]
    kept = kept.reshape(cd_tiles, peers, own_cols).transpose(1, 0, 2)
    need = doubling_max(jnp.max(jnp.sum(kept, axis=(1, 2))), "vir")
    dense = cd_tiles * own_cols
    flat = kept.reshape(peers, dense)
    rank = jnp.cumsum(flat, axis=1) - 1
    hit = flat[:, None, :] & (rank[:, None, :] == jnp.arange(dense)[None, :, None])
    slot = jnp.sum(hit * jnp.arange(dense), axis=2)
    valid = jnp.any(hit, axis=2)
    order = slot // own_cols
    col_of = jnp.arange(peers)[:, None] * own_cols + slot % own_cols
    me = lax.axis_index("occ")
    blocks = integrals.reshape(cd_tiles, tile_edge, own_cols * tile_edge)[order[me]]
    int_kept = blocks[:, :, :tile_edge]
    for col in range(1, own_cols):
        pick = (slot[me] % own_cols == col)[:, None, None]
        int_kept = jnp.where(pick, blocks[:, :, col * tile_edge:(col + 1) * tile_edge], int_kept)
    row_for_q = jnp.argmax(occ_sym[:, None] == cd_sym[None, :], axis=0)
    lam4 = lam.reshape(row_tiles, tile_edge, cd_tiles, tile_edge)
    pick = (row_for_q[None, :] == jnp.arange(row_tiles)[:, None])[:, None, :, None]
    lam_kept = jnp.sum(jnp.where(pick, lam4, jnp.zeros((), lam.dtype)), axis=0)
    lam_kept = lam_kept.transpose(1, 0, 2)
    caps = sorted({max(1, dense // 3), max(1, dense // 2), dense})
    branch = sum((need > cap).astype(jnp.int32) for cap in caps[:-1])
    partial_sum = lax.switch(
        branch,
        [
            lambda l, i, cap=cap: packed_partials(l, i, order, valid, col_of, col_tiles, cap)
            for cap in caps
        ],
        lam_kept,
        int_kept,
    )
    summed = halving_reduce_scatter(partial_sum, "vir")
    own_row = row_of[lax.axis_index("vir")]
    keep = (jnp.arange(row_tiles) == own_row)[:, None, None]
    out = jnp.where(keep, summed.astype(jnp.bfloat16)[None], jnp.zeros((), jnp.bfloat16))
    return out.reshape(row_tiles * tile_edge, summed.shape[1])


def solution(mesh):
    in_specs = (P("occ", "vir"), P("vir", "occ"), P("occ"), P("vir"), P())
    out_specs = P("occ", "vir")
    return jax.shard_map(
        on_device, mesh=mesh, in_specs=in_specs, out_specs=out_specs, check_vma=False
    )
```

profile of v0, /device:TPU:0, one launch (start us, length us, event | category | flops | bytes accessed | tf_op | source)
XLA Modules:
  0.0 92.5 jit_solution(9404032692386627359)
XLA Ops:
  6.5 0.8 eq.168
  7.4 0.7 fusion.42
  9.4 0.7 eq.171
  10.6 0.7 fusion.40
  11.3 4.7 %copy.46 = bf16[1024,1536]{0,1:T(8,128)(2,1)} copy(bf16[1024,1536]{1,0:T(8,128)(2,1)} %param.8) | data formatting | bytes 6291456 | tf_op args[0]
  15.9 4.4 %copy.52 = bf16[192,8,8,128]{3,2,1,0:T(8,128)(2,1)} copy(bf16[192,8,8,128]{3,1,2,0:T(8,128)(2,1)} %bitcast.66) | data formatting | bytes 6291456
  21.2 4.1 %select_reduce_fusion = bf16[128,12,128]{0,2,1:T(8,128)(2,1)S(1)} fusion(bf16[8,128,12,128]{1,0,3,2:T(8,128)(2,1)} %bitcast.65, pred[8,12]{0,1:T(8,128)(4,1)S(1)} %iota_compare_fusion.4), kind=kLoop, calls=%fused_computation.49 | loop fusion | flops 2949120 | bytes 3539040 | tf_op jit(solution)/shard_map/reduce_sum | solution.py:75
  27.3 3.9 %collective-permute-start.1 = (s32[]{:T(128)}, s32[]{:T(128)}, u32[]{:S(2)}, u32[]{:S(2)}) collective-permute-start(s32[]{:T(128)} %max.9), channel_id=1, source_target_pairs={{0,2},{1,3},{2,0},{3,1},{4,6},{5,7},{6,4},{7,5},{8,10},{9,11},{10,... | collective-permute-start | bytes 20 | tf_op jit(solution)/shard_map/ppermute | solution.py:26
  32.0 3.4 %collective-permute-start.2 = (s32[]{:T(128)}, s32[]{:T(128)}, u32[]{:S(2)}, u32[]{:S(2)}) collective-permute-start(s32[]{:T(128)} %max.10), channel_id=1, source_target_pairs={{0,4},{1,5},{2,6},{3,7},{4,0},{5,1},{6,2},{7,3},{8,12},{9,13},{10,... | collective-permute-start | bytes 20 | tf_op jit(solution)/shard_map/ppermute | solution.py:26
  36.3 36.0 %conditional.1 = (f32[4,2,128,128]{3,1,0,2:T(2,128)S(1)}) conditional(s32[]{:T(128)} %clamp.3, (s32[4,24]{1,0:T(4,128)S(1)}, pred[4,24]{1,0:T(4,128)(4,1)}, s32[4,24]{1,0:T(4,128)S(1)}, bf16[12,128,128]{1,2,0:T(8,128)(2,1)S(1)}, bf16[24,128,128]{2,1,0:T(8,128)(2,1)S(1)}) %tuple.44, (s32[4,24]{1,0:T(4,128)S(1)}, ...), branch_computations={%region_8.9_spmd, %region_9.10_spmd, %region_10.11_spmd} | conditional | flops 555223808 | bytes 41426764 | solution.py:79
  36.4 0.7 slice.23
  37.5 0.7 and.71
  38.3 0.7 gather_fusion
  39.0 29.4 %all-gather.4.cloned.1.call-done = bf16[32,128,128]{2,1,0:T(8,128)(2,1)} async-done(((bf16[8,128,128]{2,1,0:T(8,128)(2,1)}), bf16[32,128,128]{2,1,0:T(8,128)(2,1)}) %all-gather.4.cloned.1.call-update) | async-done | bytes 1048592 | tf_op jit(solution)/shard_map/cond/branch_0_fun/all_gather | solution.py:33
  68.5 1.7 %fusion.2 = f32[32,128,128]{2,1,0:T(8,128)S(1)} fusion(bf16[32,128,128]{2,1,0:T(8,128)(2,1)} %all-gather.4.cloned.1.call-done, bf16[32,128,128]{2,1,0:T(8,128)(2,1)S(1)} %gather_fusion, pred[32]{0:T(512)(128)(4,1)S(1)} %and.71), kind=kOutput, calls=%fused_computation.6 | convolution fusion | flops 134742016 | bytes 4194336 | tf_op jit(solution)/shard_map/cond/branch_0_fun/srm,smc->src/dot_general | solution.py:38
  70.2 2.0 %fusion = f32[8,128,128]{2,0,1:T(8,128)S(1)} fusion(f32[32,128,128]{2,1,0:T(8,128)S(1)} %fusion.2, s32[32]{0:T(128)S(1)} %eq.88, pred[32]{0:T(512)(128)(4,1)S(1)} %and.71), kind=kOutput, calls=%fused_computation.4 | convolution fusion | flops 50332160 | bytes 2621600 | tf_op jit(solution)/shard_map/cond/branch_0_fun/ts,src->trc/dot_general | solution.py:42
  73.0 1.5 %collective-permute-done.3 = f32[4,128,128]{2,0,1:T(4,128)S(1)} collective-permute-done((f32[4,128,128]{2,0,1:T(4,128)S(1)}, f32[4,128,128]{2,0,1:T(4,128)S(1)}, u32[]{:S(2)}, u32[]{:S(2)}) %collective-permute-start.3) | collective-permute-done | bytes 262176 | tf_op jit(solution)/shard_map/ppermute | solution.py:17
  74.8 1.5 %collective-permute-start.4 = (f32[2,128,128]{2,1,0:T(8,128)S(1)}, f32[2,128,128]{2,1,0:T(8,128)S(1)}, u32[]{:S(2)}, u32[]{:S(2)}) collective-permute-start(f32[2,128,128]{2,1,0:T(8,128)S(1)} %bitcast.76), channel_id=1, source_target_pairs={{0,2},{1,3},{2,0},{3,1},{4,6},{5,7},{6,4},{7,5},{8,10},{9,11},{10,... | collective-permute-start | bytes 393224 | tf_op jit(solution)/shard_map/ppermute | solution.py:17
  76.3 0.7 iota_reduce_fusion.1
  77.6 0.6 iota_compare_fusion.5
  78.3 2.1 %collective-permute-done.4 = f32[2,128,128]{2,1,0:T(8,128)S(1)} collective-permute-done((f32[2,128,128]{2,1,0:T(8,128)S(1)}, f32[2,128,128]{2,1,0:T(8,128)S(1)}, u32[]{:S(2)}, u32[]{:S(2)}) %collective-permute-start.4) | collective-permute-done | bytes 131104 | tf_op jit(solution)/shard_map/ppermute | solution.py:17
  80.4 1.5 %collective-permute-start.5 = (f32[1,128,128]{2,1,0:T(8,128)S(1)}, f32[1,128,128]{2,1,0:T(8,128)S(1)}, u32[]{:S(2)}, u32[]{:S(2)}) collective-permute-start(f32[1,128,128]{2,1,0:T(8,128)S(1)} %constant_dynamic-slice_fusion.6), channel_id=1, source_target_pairs={{0,4},{1,5},{2,6},{3,7},{4,0},{5,1},{6,2},{7,3},{8,12},{9,13},{10,... | collective-permute-start | bytes 196616 | tf_op jit(solution)/shard_map/ppermute | solution.py:17
  82.0 2.7 %collective-permute-done.5 = f32[1,128,128]{2,1,0:T(8,128)S(1)} collective-permute-done((f32[1,128,128]{2,1,0:T(8,128)S(1)}, f32[1,128,128]{2,1,0:T(8,128)S(1)}, u32[]{:S(2)}, u32[]{:S(2)}) %collective-permute-start.5) | collective-permute-done | bytes 65568 | tf_op jit(solution)/shard_map/ppermute | solution.py:17
  84.8 0.9 bitcast_select_fusion
  (47 shorter events, 5.7 us)
Async XLA Ops:
  6.5 18.7 %copy-start = (bf16[1536,256]{1,0:T(8,128)(2,1)S(1)}, bf16[1536,256]{1,0:T(8,128)(2,1)}, u32[]{:S(2)}) copy-start(bf16[1536,256]{1,0:T(8,128)(2,1)} %param.9) | copy-start | bytes 2359300
  8.8 17.3 %collective-permute-start = (s32[]{:T(128)}, s32[]{:T(128)}, u32[]{:S(2)}, u32[]{:S(2)}) collective-permute-start(s32[]{:T(128)} %reduce_max.9), channel_id=1, source_target_pairs={{0,1},{1,0},{2,3},{3,2},{4,5},{5,4},{6,7},{7,6},{8,9},{9,8},{10,11... | collective-permute-start | bytes 20 | tf_op jit(solution)/shard_map/ppermute | solution.py:26
  15.9 4.4 %copy-start.2 = (s32[12]{0:T(128)S(1)}, s32[12]{0:T(128)}, u32[]{:S(2)}) copy-start(s32[12]{0:T(128)} %param.11) | copy-start | bytes 148
  15.9 4.4 %copy-start.4 = (s32[8]{0:T(128)S(1)}, s32[8]{0:T(128)}, u32[]{:S(2)}) copy-start(s32[8]{0:T(128)} %param.10) | copy-start | bytes 100
  27.3 4.0 %collective-permute-start.1 = (s32[]{:T(128)}, s32[]{:T(128)}, u32[]{:S(2)}, u32[]{:S(2)}) collective-permute-start(s32[]{:T(128)} %max.9), channel_id=1, source_target_pairs={{0,2},{1,3},{2,0},{3,1},{4,6},{5,7},{6,4},{7,5},{8,10},{9,11},{10,... | collective-permute-start | bytes 20 | tf_op jit(solution)/shard_map/ppermute | solution.py:26
  32.0 3.6 %collective-permute-start.2 = (s32[]{:T(128)}, s32[]{:T(128)}, u32[]{:S(2)}, u32[]{:S(2)}) collective-permute-start(s32[]{:T(128)} %max.10), channel_id=1, source_target_pairs={{0,4},{1,5},{2,6},{3,7},{4,0},{5,1},{6,2},{7,3},{8,12},{9,13},{10,... | collective-permute-start | bytes 20 | tf_op jit(solution)/shard_map/ppermute | solution.py:26
  36.3 40.0 %copy-start.3 = (s32[8]{0:T(128)S(1)}, s32[8]{0:T(128)}, u32[]{:S(2)}) copy-start(s32[8]{0:T(128)} %param.12) | copy-start | bytes 100
  36.4 32.1 %all-gather.4.cloned.1.call-start = ((), (), s32[]{:S(2)}) async-start(), calls=%async_computation | async-start | bytes 1310720 | tf_op jit(solution)/shard_map/cond/branch_0_fun/all_gather | solution.py:33
  72.9 1.6 %collective-permute-start.3 = (f32[4,128,128]{2,0,1:T(4,128)S(1)}, f32[4,128,128]{2,0,1:T(4,128)S(1)}, u32[]{:S(2)}, u32[]{:S(2)}) collective-permute-start(f32[4,128,128]{2,0,1:T(4,128)S(1)} %bitcast.75), channel_id=1, source_target_pairs={{0,1},{1,0},{2,3},{3,2},{4,5},{5,4},{6,7},{7,6},{8,9},{9,8},{10,11... | collective-permute-start | bytes 786440 | tf_op jit(solution)/shard_map/ppermute | solution.py:17
  74.8 5.6 %collective-permute-start.4 = (f32[2,128,128]{2,1,0:T(8,128)S(1)}, f32[2,128,128]{2,1,0:T(8,128)S(1)}, u32[]{:S(2)}, u32[]{:S(2)}) collective-permute-start(f32[2,128,128]{2,1,0:T(8,128)S(1)} %bitcast.76), channel_id=1, source_target_pairs={{0,2},{1,3},{2,0},{3,1},{4,6},{5,7},{6,4},{7,5},{8,10},{9,11},{10,... | collective-permute-start | bytes 393224 | tf_op jit(solution)/shard_map/ppermute | solution.py:17
  80.4 4.3 %collective-permute-start.5 = (f32[1,128,128]{2,1,0:T(8,128)S(1)}, f32[1,128,128]{2,1,0:T(8,128)S(1)}, u32[]{:S(2)}, u32[]{:S(2)}) collective-permute-start(f32[1,128,128]{2,1,0:T(8,128)S(1)} %constant_dynamic-slice_fusion.6), channel_id=1, source_target_pairs={{0,4},{1,5},{2,6},{3,7},{4,0},{5,1},{6,2},{7,3},{8,12},{9,13},{10,... | collective-permute-start | bytes 196616 | tf_op jit(solution)/shard_map/ppermute | solution.py:17
Sparse Core Ops, SparseCore 0:
  38.8 29.6 all-gather.3
where the time goes:
time: 92.9 us; the launch traced here: 92.5 us
  waiting for transfers between devices  36.1 us (39%)
  between operations  16.2 us (17%)
  local copies, waits for them, and re-layouts  15.5 us (17%)
  starting transfers between devices  10.9 us (12%)
  other arithmetic  9.83 us (11%)
  matrix products  3.67 us (4%)
    all_gather x1, waiting for transfers between devices, packed_partials(): received = lax.all_gather(int_kept[:cap], 'occ', axis=0, tiled=True)  29.4 us
    unnamed x10, local copies, waits for them, and re-layouts  9.11 us
    ppermute x3, starting transfers between devices, doubling_max(): lax.ppermute(value, axis, [(j, j ^ step) for j in range(n)])  7.71 us
    ppermute x3, waiting for transfers between devices, halving_reduce_scatter(): parts = keep + lax.ppermute(send, axis, perm)  6.33 us
    reduce_sum x1, other arithmetic, on_device(): lam_kept = jnp.sum(jnp.where(pick, lam4, jnp.zeros((), lam.dtype)), axis=0)  4.06 us
    ppermute x3, starting transfers between devices, halving_reduce_scatter(): parts = keep + lax.ppermute(send, axis, perm)  3.14 us
    dot_general x1, matrix products, packed_partials(): jnp.einsum('ts,src->trc', owner.astype(jnp.float32), products, precision=...  1.96 us
  transfers between devices with their start and end apart: 7, of which 6 were waited for; matrix products, arithmetic and copies ran while one was open for 22% of the time, Pallas kernels for 0%

commit v1 on v0

--- a/solution.py
+++ b/solution.py
@@ -70,10 +70,10 @@
         pick = (slot[me] % own_cols == col)[:, None, None]
         int_kept = jnp.where(pick, blocks[:, :, col * tile_edge:(col + 1) * tile_edge], int_kept)
     row_for_q = jnp.argmax(occ_sym[:, None] == cd_sym[None, :], axis=0)
-    lam4 = lam.reshape(row_tiles, tile_edge, cd_tiles, tile_edge)
-    pick = (row_for_q[None, :] == jnp.arange(row_tiles)[:, None])[:, None, :, None]
-    lam_kept = jnp.sum(jnp.where(pick, lam4, jnp.zeros((), lam.dtype)), axis=0)
-    lam_kept = lam_kept.transpose(1, 0, 2)
+    lam3 = lam.reshape(row_tiles, tile_edge, cd_tiles * tile_edge)
+    pick = jnp.repeat(row_for_q[None, :] == jnp.arange(row_tiles)[:, None], tile_edge, axis=1)
+    lam_kept = jnp.sum(jnp.where(pick[:, None, :], lam3, jnp.zeros((), lam.dtype)), axis=0)
+    lam_kept = lam_kept.reshape(tile_edge, cd_tiles, tile_edge).transpose(1, 0, 2)
     caps = sorted({max(1, dense // 3), max(1, dense // 2), dense})
     branch = sum((need > cap).astype(jnp.int32) for cap in caps[:-1])
     partial_sum = lax.switch(

time: 92.9 us -> 82.9 us (0.89)
  local copies, waits for them, and re-layouts: 15.5 us -> 6.08 us
  other arithmetic: 9.83 us -> 8.56 us
    unnamed x10 -> x6, local copies, waits for them, and re-layouts: 9.11 us -> 0.02 us
    reduce_sum x1, other arithmetic: 4.06 us -> 2.7 us  [on_device(): jnp.sum(jnp.where(pick[:, None, :], lam3, jnp.zeros((), lam.dtype)), axis=0)]
  transfers between devices with their start and end apart: 7 -> 7, of which waited for: 6 -> 6; matrix products, arithmetic and copies ran while one was open for 22% -> 12% of each run, Pallas kernels for 0% -> 0%
where the time goes in v1:
time: 82.9 us; the launch traced here: 82.6 us
  waiting for transfers between devices  36.8 us (44%)
  between operations  16.4 us (20%)
  starting transfers between devices  10.9 us (13%)
  other arithmetic  8.56 us (10%)
  local copies, waits for them, and re-layouts  6.08 us (7%)
  matrix products  3.67 us (4%)
    all_gather x1, waiting for transfers between devices, packed_partials(): received = lax.all_gather(int_kept[:cap], 'occ', axis=0, tiled=True)  30.1 us
    ppermute x3, starting transfers between devices, doubling_max(): lax.ppermute(value, axis, [(j, j ^ step) for j in range(n)])  7.71 us
    ppermute x3, waiting for transfers between devices, halving_reduce_scatter(): parts = keep + lax.ppermute(send, axis, perm)  6.33 us
    ppermute x3, starting transfers between devices, halving_reduce_scatter(): parts = keep + lax.ppermute(send, axis, perm)  3.14 us
    reduce_sum x1, other arithmetic, on_device(): jnp.sum(jnp.where(pick[:, None, :], lam3, jnp.zeros((), lam.dtype)), axis=0)  2.7 us
    dot_general x1, matrix products, packed_partials(): jnp.einsum('ts,src->trc', owner.astype(jnp.float32), products, precision=...  1.96 us
    eq x6, local copies, waits for them, and re-layouts, on_device(): kept = cd_sym[:, None] == ab_sym[None, :]  1.8 us
    dot_general x1, matrix products, packed_partials(): jnp.einsum('srm,smc->src', lam_tiles, received, preferred_element_type=jn...  1.71 us
  transfers between devices with their start and end apart: 7, of which 6 were waited for; matrix products, arithmetic and copies ran while one was open for 12% of the time, Pallas kernels for 0%

profile of v1, /device:TPU:0, one launch (start us, length us, event | category | flops | bytes accessed | tf_op | source)
XLA Modules:
  0.0 82.6 jit_solution(15122857072546760054)
XLA Ops:
  6.5 0.8 eq.164
  7.4 0.7 fusion.42
  8.2 0.6 reduce_max.9
  9.4 0.7 eq.167
  10.7 1.3 %iota_reduce_fusion = (pred[12]{0:T(512)(128)(4,1)}, s32[12]{0:T(128)S(1)}) fusion(s32[12]{0:T(128)} %param.11, s32[8]{0:T(128)} %param.10), kind=kLoop, calls=%fused_computation.65 | loop fusion | flops 684 | bytes 140 | tf_op jit(solution)/shard_map/on_device/reduce | solution.py:72
  12.2 2.7 %select_reduce_fusion = bf16[128,1536]{1,0:T(8,128)(2,1)S(1)} fusion(bf16[8,128,1536]{2,1,0:T(8,128)(2,1)} %bitcast.68, pred[8,1536]{1,0:T(8,128)(4,1)S(1)} %broadcast_bitcast_fusion), kind=kLoop, calls=%fused_computation.49 | loop fusion | flops 2949120 | bytes 3551232 | tf_op jit(solution)/shard_map/reduce_sum | solution.py:75
  15.2 0.6 gather_fusion.3
  17.4 3.9 %collective-permute-start.1 = (s32[]{:T(128)}, s32[]{:T(128)}, u32[]{:S(2)}, u32[]{:S(2)}) collective-permute-start(s32[]{:T(128)} %max.9), channel_id=1, source_target_pairs={{0,2},{1,3},{2,0},{3,1},{4,6},{5,7},{6,4},{7,5},{8,10},{9,11},{10,... | collective-permute-start | bytes 20 | tf_op jit(solution)/shard_map/ppermute | solution.py:26
  22.1 3.4 %collective-permute-start.2 = (s32[]{:T(128)}, s32[]{:T(128)}, u32[]{:S(2)}, u32[]{:S(2)}) collective-permute-start(s32[]{:T(128)} %max.10), channel_id=1, source_target_pairs={{0,4},{1,5},{2,6},{3,7},{4,0},{5,1},{6,2},{7,3},{8,12},{9,13},{10,... | collective-permute-start | bytes 20 | tf_op jit(solution)/shard_map/ppermute | solution.py:26
  26.4 36.0 %conditional.1 = (f32[4,2,128,128]{3,1,0,2:T(2,128)S(1)}) conditional(s32[]{:T(128)} %clamp.3, (s32[4,24]{1,0:T(4,128)S(1)}, pred[4,24]{1,0:T(4,128)(4,1)S(1)}, s32[4,24]{1,0:T(4,128)S(1)}, bf16[12,128,128]{1,2,0:T(8,128)(2,1)S(1)}, bf16[24,128,128]{2,1,0:T(8,128)(2,1)S(1)}) %tuple.47, (s32[4,24]{1,0:T(4,128)S(1)}, ...), branch_computations={%region_8.9_spmd, %region_9.10_spmd, %region_10.11_spmd} | conditional | flops 555223808 | bytes 41426764 | solution.py:79
  26.5 0.7 slice.23
  27.8 0.7 gather_fusion
  28.5 30.1 %all-gather.4.cloned.1.call-done = bf16[32,128,128]{2,1,0:T(8,128)(2,1)} async-done(((bf16[8,128,128]{2,1,0:T(8,128)(2,1)}), bf16[32,128,128]{2,1,0:T(8,128)(2,1)}) %all-gather.4.cloned.1.call-update) | async-done | bytes 1048592 | tf_op jit(solution)/shard_map/cond/branch_0_fun/all_gather | solution.py:33
  58.6 1.7 %fusion.2 = f32[32,128,128]{2,1,0:T(8,128)S(1)} fusion(bf16[32,128,128]{2,1,0:T(8,128)(2,1)} %all-gather.4.cloned.1.call-done, bf16[32,128,128]{2,1,0:T(8,128)(2,1)S(1)} %gather_fusion, pred[32]{0:T(512)(128)(4,1)S(1)} %and.71), kind=kOutput, calls=%fused_computation.6 | convolution fusion | flops 134742016 | bytes 4194336 | tf_op jit(solution)/shard_map/cond/branch_0_fun/srm,smc->src/dot_general | solution.py:38
  60.3 2.0 %fusion = f32[8,128,128]{2,0,1:T(8,128)S(1)} fusion(f32[32,128,128]{2,1,0:T(8,128)S(1)} %fusion.2, s32[32]{0:T(128)S(1)} %eq.76, pred[32]{0:T(512)(128)(4,1)S(1)} %and.71), kind=kOutput, calls=%fused_computation.4 | convolution fusion | flops 50332160 | bytes 2621600 | tf_op jit(solution)/shard_map/cond/branch_0_fun/ts,src->trc/dot_general | solution.py:42
  63.1 1.5 %collective-permute-done.3 = f32[4,128,128]{2,0,1:T(4,128)S(1)} collective-permute-done((f32[4,128,128]{2,0,1:T(4,128)S(1)}, f32[4,128,128]{2,0,1:T(4,128)S(1)}, u32[]{:S(2)}, u32[]{:S(2)}) %collective-permute-start.3) | collective-permute-done | bytes 262176 | tf_op jit(solution)/shard_map/ppermute | solution.py:17
  64.9 1.5 %collective-permute-start.4 = (f32[2,128,128]{2,1,0:T(8,128)S(1)}, f32[2,128,128]{2,1,0:T(8,128)S(1)}, u32[]{:S(2)}, u32[]{:S(2)}) collective-permute-start(f32[2,128,128]{2,1,0:T(8,128)S(1)} %bitcast.75), channel_id=1, source_target_pairs={{0,2},{1,3},{2,0},{3,1},{4,6},{5,7},{6,4},{7,5},{8,10},{9,11},{10,... | collective-permute-start | bytes 393224 | tf_op jit(solution)/shard_map/ppermute | solution.py:17
  66.4 0.7 iota_reduce_fusion.1
  67.1 0.6 dynamic_slice.26
  67.7 0.6 iota_compare_fusion.5
  68.4 2.1 %collective-permute-done.4 = f32[2,128,128]{2,1,0:T(8,128)S(1)} collective-permute-done((f32[2,128,128]{2,1,0:T(8,128)S(1)}, f32[2,128,128]{2,1,0:T(8,128)S(1)}, u32[]{:S(2)}, u32[]{:S(2)}) %collective-permute-start.4) | collective-permute-done | bytes 131104 | tf_op jit(solution)/shard_map/ppermute | solution.py:17
  70.5 1.5 %collective-permute-start.5 = (f32[1,128,128]{2,1,0:T(8,128)S(1)}, f32[1,128,128]{2,1,0:T(8,128)S(1)}, u32[]{:S(2)}, u32[]{:S(2)}) collective-permute-start(f32[1,128,128]{2,1,0:T(8,128)S(1)} %constant_dynamic-slice_fusion.6), channel_id=1, source_target_pairs={{0,4},{1,5},{2,6},{3,7},{4,0},{5,1},{6,2},{7,3},{8,12},{9,13},{10,... | collective-permute-start | bytes 196616 | tf_op jit(solution)/shard_map/ppermute | solution.py:17
  72.1 2.7 %collective-permute-done.5 = f32[1,128,128]{2,1,0:T(8,128)S(1)} collective-permute-done((f32[1,128,128]{2,1,0:T(8,128)S(1)}, f32[1,128,128]{2,1,0:T(8,128)S(1)}, u32[]{:S(2)}, u32[]{:S(2)}) %collective-permute-start.5) | collective-permute-done | bytes 65568 | tf_op jit(solution)/shard_map/ppermute | solution.py:17
  74.9 0.9 %bitcast_select_fusion = bf16[1024,128]{1,0:T(8,128)(2,1)} fusion(pred[1024]{0:T(1024)(128)(4,1)S(1)} %broadcast_bitcast_fusion.1, bf16[128,128]{1,0:T(8,128)(2,1)S(1)} %fusion.41), kind=kLoop, calls=%fused_computation.51 | loop fusion | flops 131072 | bytes 295936 | tf_op jit(solution)/shard_map/jit(_where)/select_n | solution.py:91
  (45 shorter events, 3.7 us)
Async XLA Ops:
  6.5 8.7 %copy-start = (bf16[1536,256]{1,0:T(8,128)(2,1)S(1)}, bf16[1536,256]{1,0:T(8,128)(2,1)}, u32[]{:S(2)}) copy-start(bf16[1536,256]{1,0:T(8,128)(2,1)} %param.9) | copy-start | bytes 2359300
  8.8 7.2 %collective-permute-start = (s32[]{:T(128)}, s32[]{:T(128)}, u32[]{:S(2)}, u32[]{:S(2)}) collective-permute-start(s32[]{:T(128)} %reduce_max.9), channel_id=1, source_target_pairs={{0,1},{1,0},{2,3},{3,2},{4,5},{5,4},{6,7},{7,6},{8,9},{9,8},{10,11... | collective-permute-start | bytes 20 | tf_op jit(solution)/shard_map/ppermute | solution.py:26
  17.4 4.0 %collective-permute-start.1 = (s32[]{:T(128)}, s32[]{:T(128)}, u32[]{:S(2)}, u32[]{:S(2)}) collective-permute-start(s32[]{:T(128)} %max.9), channel_id=1, source_target_pairs={{0,2},{1,3},{2,0},{3,1},{4,6},{5,7},{6,4},{7,5},{8,10},{9,11},{10,... | collective-permute-start | bytes 20 | tf_op jit(solution)/shard_map/ppermute | solution.py:26
  22.1 3.6 %collective-permute-start.2 = (s32[]{:T(128)}, s32[]{:T(128)}, u32[]{:S(2)}, u32[]{:S(2)}) collective-permute-start(s32[]{:T(128)} %max.10), channel_id=1, source_target_pairs={{0,4},{1,5},{2,6},{3,7},{4,0},{5,1},{6,2},{7,3},{8,12},{9,13},{10,... | collective-permute-start | bytes 20 | tf_op jit(solution)/shard_map/ppermute | solution.py:26
  26.4 40.0 %copy-start.2 = (s32[8]{0:T(128)S(1)}, s32[8]{0:T(128)}, u32[]{:S(2)}) copy-start(s32[8]{0:T(128)} %param.12) | copy-start | bytes 100
  26.4 40.0 %copy-start.3 = (s32[8]{0:T(128)S(1)}, s32[8]{0:T(128)}, u32[]{:S(2)}) copy-start(s32[8]{0:T(128)} %param.10) | copy-start | bytes 100
  26.4 32.1 %all-gather.4.cloned.1.call-start = ((), (), s32[]{:S(2)}) async-start(), calls=%async_computation | async-start | bytes 1310720 | tf_op jit(solution)/shard_map/cond/branch_0_fun/all_gather | solution.py:33
  62.9 1.6 %collective-permute-start.3 = (f32[4,128,128]{2,0,1:T(4,128)S(1)}, f32[4,128,128]{2,0,1:T(4,128)S(1)}, u32[]{:S(2)}, u32[]{:S(2)}) collective-permute-start(f32[4,128,128]{2,0,1:T(4,128)S(1)} %bitcast.74), channel_id=1, source_target_pairs={{0,1},{1,0},{2,3},{3,2},{4,5},{5,4},{6,7},{7,6},{8,9},{9,8},{10,11... | collective-permute-start | bytes 786440 | tf_op jit(solution)/shard_map/ppermute | solution.py:17
  64.9 5.6 %collective-permute-start.4 = (f32[2,128,128]{2,1,0:T(8,128)S(1)}, f32[2,128,128]{2,1,0:T(8,128)S(1)}, u32[]{:S(2)}, u32[]{:S(2)}) collective-permute-start(f32[2,128,128]{2,1,0:T(8,128)S(1)} %bitcast.75), channel_id=1, source_target_pairs={{0,2},{1,3},{2,0},{3,1},{4,6},{5,7},{6,4},{7,5},{8,10},{9,11},{10,... | collective-permute-start | bytes 393224 | tf_op jit(solution)/shard_map/ppermute | solution.py:17
  70.5 4.3 %collective-permute-start.5 = (f32[1,128,128]{2,1,0:T(8,128)S(1)}, f32[1,128,128]{2,1,0:T(8,128)S(1)}, u32[]{:S(2)}, u32[]{:S(2)}) collective-permute-start(f32[1,128,128]{2,1,0:T(8,128)S(1)} %constant_dynamic-slice_fusion.6), channel_id=1, source_target_pairs={{0,4},{1,5},{2,6},{3,7},{4,0},{5,1},{6,2},{7,3},{8,12},{9,13},{10,... | collective-permute-start | bytes 196616 | tf_op jit(solution)/shard_map/ppermute | solution.py:17
Sparse Core Ops, SparseCore 0:
  28.9 29.6 all-gather.3

commit v2 on v1

--- a/solution.py
+++ b/solution.py
@@ -54,7 +54,7 @@
     row_of = jnp.argmax(occ_sym[None, :] == ab_sym[:, None], axis=1)
     kept = cd_sym[:, None] == ab_sym[None, :]
     kept = kept.reshape(cd_tiles, peers, own_cols).transpose(1, 0, 2)
-    need = doubling_max(jnp.max(jnp.sum(kept, axis=(1, 2))), "vir")
+    need = lax.pmax(jnp.max(jnp.sum(kept, axis=(1, 2))), "vir")
     dense = cd_tiles * own_cols
     flat = kept.reshape(peers, dense)
     rank = jnp.cumsum(flat, axis=1) - 1

time: 82.9 us -> 81.4 us (0.982)
  blocking collectives: 0 us -> 10.1 us
  starting transfers between devices: 10.9 us -> 3.19 us
  waiting for transfers between devices: 36.8 us -> 34.3 us
  between operations: 16.4 us -> 14.9 us
    pmax x0 -> x1, blocking collectives: none -> 10.1 us  [on_device(): need = lax.pmax(jnp.max(jnp.sum(kept, axis=(1, 2))), 'vir')]
    ppermute x3 -> x0, starting transfers between devices: 7.71 us -> none  [doubling_max(): lax.ppermute(value, axis, [(j, j ^ step) for j in range(n)])]
    all_gather x1, waiting for transfers between devices: 30.1 us -> 28 us  [packed_partials(): received = lax.all_gather(int_kept[:cap], 'occ', axis=0, tiled=True)]
  transfers between devices with their start and end apart: 7 -> 4, of which waited for: 6 -> 4; matrix products, arithmetic and copies ran while one was open for 12% -> 4% of each run, Pallas kernels for 0% -> 0%
where the time goes in v2:
time: 81.4 us; the launch traced here: 81.1 us
  waiting for transfers between devices  34.3 us (42%)
  between operations  14.9 us (18%)
  blocking collectives  10.1 us (12%)
  other arithmetic  8.56 us (11%)
  local copies, waits for them, and re-layouts  6.07 us (7%)
  matrix products  3.67 us (5%)
  starting transfers between devices  3.19 us (4%)
    all_gather x1, waiting for transfers between devices, packed_partials(): received = lax.all_gather(int_kept[:cap], 'occ', axis=0, tiled=True)  28 us
    pmax x1, blocking collectives, on_device(): need = lax.pmax(jnp.max(jnp.sum(kept, axis=(1, 2))), 'vir')  10.1 us
    ppermute x3, waiting for transfers between devices, halving_reduce_scatter(): parts = keep + lax.ppermute(send, axis, perm)  6.33 us
    ppermute x3, starting transfers between devices, halving_reduce_scatter(): parts = keep + lax.ppermute(send, axis, perm)  3.15 us
    reduce_sum x1, other arithmetic, on_device(): jnp.sum(jnp.where(pick[:, None, :], lam3, jnp.zeros((), lam.dtype)), axis=0)  2.7 us
    dot_general x1, matrix products, packed_partials(): jnp.einsum('ts,src->trc', owner.astype(jnp.float32), products, precision=...  1.96 us
    eq x6, local copies, waits for them, and re-layouts, on_device(): kept = cd_sym[:, None] == ab_sym[None, :]  1.8 us
    dot_general x1, matrix products, packed_partials(): jnp.einsum('srm,smc->src', lam_tiles, received, preferred_element_type=jn...  1.71 us
  transfers between devices with their start and end apart: 4, of which 4 were waited for; matrix products, arithmetic and copies ran while one was open for 4% of the time, Pallas kernels for 0%

profile of v2, /device:TPU:0, one launch (start us, length us, event | category | flops | bytes accessed | tf_op | source)
XLA Modules:
  0.0 81.1 jit_solution(4339488879119234323)
XLA Ops:
  6.5 0.8 eq.164
  7.4 0.7 fusion.42
  8.3 0.7 eq.167
  9.6 0.6 reduce_max.9
  10.3 10.1 %pmax.7 = s32[]{:T(128)} all-reduce(s32[]{:T(128)} %reduce_max.9), channel_id=1, replica_groups=mesh['occ'=4,'vir'=8] {'vir'}, use_global_device_ids=true, to_apply=%region_3.4 | all-reduce | flops 1 | bytes 8 | tf_op jit(solution)/shard_map/pmax | solution.py:57
  21.7 1.3 %iota_reduce_fusion = (pred[12]{0:T(512)(128)(4,1)}, s32[12]{0:T(128)S(1)}) fusion(s32[12]{0:T(128)} %param.11, s32[8]{0:T(128)} %param.10), kind=kLoop, calls=%fused_computation.65 | loop fusion | flops 684 | bytes 140 | tf_op jit(solution)/shard_map/on_device/reduce | solution.py:72
  23.1 2.7 %select_reduce_fusion = bf16[128,1536]{1,0:T(8,128)(2,1)S(1)} fusion(bf16[8,128,1536]{2,1,0:T(8,128)(2,1)} %bitcast.68, pred[8,1536]{1,0:T(8,128)(4,1)S(1)} %broadcast_bitcast_fusion), kind=kLoop, calls=%fused_computation.49 | loop fusion | flops 2949120 | bytes 3551232 | tf_op jit(solution)/shard_map/reduce_sum | solution.py:75
  26.2 0.6 gather_fusion.3
  27.0 34.0 %conditional.1 = (f32[4,2,128,128]{3,1,0,2:T(2,128)S(1)}) conditional(s32[]{:T(128)} %clamp.3, (s32[4,24]{1,0:T(4,128)S(1)}, pred[4,24]{1,0:T(4,128)(4,1)S(1)}, s32[4,24]{1,0:T(4,128)S(1)}, bf16[12,128,128]{1,2,0:T(8,128)(2,1)S(1)}, bf16[24,128,128]{2,1,0:T(8,128)(2,1)S(1)}) %tuple.47, (s32[4,24]{1,0:T(4,128)S(1)}, ...), branch_computations={%region_9.10_spmd, %region_10.11_spmd, %region_11.12_spmd} | conditional | flops 555223808 | bytes 41426764 | solution.py:79
  27.1 0.7 slice.23
  28.3 0.7 gather_fusion
  29.1 28.0 %all-gather.4.cloned.1.call-done = bf16[32,128,128]{2,1,0:T(8,128)(2,1)} async-done(((bf16[8,128,128]{2,1,0:T(8,128)(2,1)}), bf16[32,128,128]{2,1,0:T(8,128)(2,1)}) %all-gather.4.cloned.1.call-update) | async-done | bytes 1048592 | tf_op jit(solution)/shard_map/cond/branch_0_fun/all_gather | solution.py:33
  57.1 1.7 %fusion.2 = f32[32,128,128]{2,1,0:T(8,128)S(1)} fusion(bf16[32,128,128]{2,1,0:T(8,128)(2,1)} %all-gather.4.cloned.1.call-done, bf16[32,128,128]{2,1,0:T(8,128)(2,1)S(1)} %gather_fusion, pred[32]{0:T(512)(128)(4,1)S(1)} %and.71), kind=kOutput, calls=%fused_computation.6 | convolution fusion | flops 134742016 | bytes 4194336 | tf_op jit(solution)/shard_map/cond/branch_0_fun/srm,smc->src/dot_general | solution.py:38
  58.8 2.0 %fusion = f32[8,128,128]{2,0,1:T(8,128)S(1)} fusion(f32[32,128,128]{2,1,0:T(8,128)S(1)} %fusion.2, s32[32]{0:T(128)S(1)} %eq.76, pred[32]{0:T(512)(128)(4,1)S(1)} %and.71), kind=kOutput, calls=%fused_computation.4 | convolution fusion | flops 50332160 | bytes 2621600 | tf_op jit(solution)/shard_map/cond/branch_0_fun/ts,src->trc/dot_general | solution.py:42
  61.0 0.5 constant_dynamic-slice_fusion.2
  61.6 1.5 %collective-permute-done = f32[4,128,128]{2,0,1:T(4,128)S(1)} collective-permute-done((f32[4,128,128]{2,0,1:T(4,128)S(1)}, f32[4,128,128]{2,0,1:T(4,128)S(1)}, u32[]{:S(2)}, u32[]{:S(2)}) %collective-permute-start) | collective-permute-done | bytes 262176 | tf_op jit(solution)/shard_map/ppermute | solution.py:17
  63.4 1.5 %collective-permute-start.1 = (f32[2,128,128]{2,1,0:T(8,128)S(1)}, f32[2,128,128]{2,1,0:T(8,128)S(1)}, u32[]{:S(2)}, u32[]{:S(2)}) collective-permute-start(f32[2,128,128]{2,1,0:T(8,128)S(1)} %bitcast.75), channel_id=1, source_target_pairs={{0,2},{1,3},{2,0},{3,1},{4,6},{5,7},{6,4},{7,5},{8,10},{9,11},{10,... | collective-permute-start | bytes 393224 | tf_op jit(solution)/shard_map/ppermute | solution.py:17
  64.9 0.7 iota_reduce_fusion.1
  65.6 0.6 dynamic_slice.26
  66.2 0.6 iota_compare_fusion.5
  66.9 2.1 %collective-permute-done.1 = f32[2,128,128]{2,1,0:T(8,128)S(1)} collective-permute-done((f32[2,128,128]{2,1,0:T(8,128)S(1)}, f32[2,128,128]{2,1,0:T(8,128)S(1)}, u32[]{:S(2)}, u32[]{:S(2)}) %collective-permute-start.1) | collective-permute-done | bytes 131104 | tf_op jit(solution)/shard_map/ppermute | solution.py:17
  69.0 1.5 %collective-permute-start.2 = (f32[1,128,128]{2,1,0:T(8,128)S(1)}, f32[1,128,128]{2,1,0:T(8,128)S(1)}, u32[]{:S(2)}, u32[]{:S(2)}) collective-permute-start(f32[1,128,128]{2,1,0:T(8,128)S(1)} %constant_dynamic-slice_fusion.6), channel_id=1, source_target_pairs={{0,4},{1,5},{2,6},{3,7},{4,0},{5,1},{6,2},{7,3},{8,12},{9,13},{10,... | collective-permute-start | bytes 196616 | tf_op jit(solution)/shard_map/ppermute | solution.py:17
  70.6 2.7 %collective-permute-done.2 = f32[1,128,128]{2,1,0:T(8,128)S(1)} collective-permute-done((f32[1,128,128]{2,1,0:T(8,128)S(1)}, f32[1,128,128]{2,1,0:T(8,128)S(1)}, u32[]{:S(2)}, u32[]{:S(2)}) %collective-permute-start.2) | collective-permute-done | bytes 65568 | tf_op jit(solution)/shard_map/ppermute | solution.py:17
  73.4 0.9 %bitcast_select_fusion = bf16[1024,128]{1,0:T(8,128)(2,1)} fusion(pred[1024]{0:T(1024)(128)(4,1)S(1)} %broadcast_bitcast_fusion.1, bf16[128,128]{1,0:T(8,128)(2,1)S(1)} %fusion.41), kind=kLoop, calls=%fused_computation.51 | loop fusion | flops 131072 | bytes 295936 | tf_op jit(solution)/shard_map/jit(_where)/select_n | solution.py:91
  (40 shorter events, 2.5 us)
Async XLA Ops:
  6.5 19.6 %copy-start = (bf16[1536,256]{1,0:T(8,128)(2,1)S(1)}, bf16[1536,256]{1,0:T(8,128)(2,1)}, u32[]{:S(2)}) copy-start(bf16[1536,256]{1,0:T(8,128)(2,1)} %param.9) | copy-start | bytes 2359300
  27.0 37.9 %copy-start.2 = (s32[8]{0:T(128)S(1)}, s32[8]{0:T(128)}, u32[]{:S(2)}) copy-start(s32[8]{0:T(128)} %param.12) | copy-start | bytes 100
  27.0 37.9 %copy-start.3 = (s32[8]{0:T(128)S(1)}, s32[8]{0:T(128)}, u32[]{:S(2)}) copy-start(s32[8]{0:T(128)} %param.10) | copy-start | bytes 100
  27.0 30.0 %all-gather.4.cloned.1.call-start = ((), (), s32[]{:S(2)}) async-start(), calls=%async_computation | async-start | bytes 1310720 | tf_op jit(solution)/shard_map/cond/branch_0_fun/all_gather | solution.py:33
  61.4 1.6 %collective-permute-start = (f32[4,128,128]{2,0,1:T(4,128)S(1)}, f32[4,128,128]{2,0,1:T(4,128)S(1)}, u32[]{:S(2)}, u32[]{:S(2)}) collective-permute-start(f32[4,128,128]{2,0,1:T(4,128)S(1)} %bitcast.74), channel_id=1, source_target_pairs={{0,1},{1,0},{2,3},{3,2},{4,5},{5,4},{6,7},{7,6},{8,9},{9,8},{10,11... | collective-permute-start | bytes 786440 | tf_op jit(solution)/shard_map/ppermute | solution.py:17
  63.4 5.6 %collective-permute-start.1 = (f32[2,128,128]{2,1,0:T(8,128)S(1)}, f32[2,128,128]{2,1,0:T(8,128)S(1)}, u32[]{:S(2)}, u32[]{:S(2)}) collective-permute-start(f32[2,128,128]{2,1,0:T(8,128)S(1)} %bitcast.75), channel_id=1, source_target_pairs={{0,2},{1,3},{2,0},{3,1},{4,6},{5,7},{6,4},{7,5},{8,10},{9,11},{10,... | collective-permute-start | bytes 393224 | tf_op jit(solution)/shard_map/ppermute | solution.py:17
  69.0 4.3 %collective-permute-start.2 = (f32[1,128,128]{2,1,0:T(8,128)S(1)}, f32[1,128,128]{2,1,0:T(8,128)S(1)}, u32[]{:S(2)}, u32[]{:S(2)}) collective-permute-start(f32[1,128,128]{2,1,0:T(8,128)S(1)} %constant_dynamic-slice_fusion.6), channel_id=1, source_target_pairs={{0,4},{1,5},{2,6},{3,7},{4,0},{5,1},{6,2},{7,3},{8,12},{9,13},{10,... | collective-permute-start | bytes 196616 | tf_op jit(solution)/shard_map/ppermute | solution.py:17
Sparse Core Ops, SparseCore 0:
  29.4 27.5 all-gather.3
